TPU v7x, 32 devices: a whole 2x2x4 slice. The times are simulated.
32 devices in a mesh: groups: 2 (over x), seq: 8 (over z, y), chan: 2 (over core).
Axes of the slice: x: 2, y: 2, z: 4, core: 2. Of those that a mesh axis runs over, the one named last changes fastest.
Arguments:
- cached_input: bfloat16 [2048, 4096], P(('groups', 'seq'), 'chan'), parts along dimension 0, may hold values from -6 to 6
- cached_gate: bfloat16 [2048, 4096], P(('groups', 'seq'), 'chan'), parts along dimension 0, may hold values from -6 to 6
- out_grad: bfloat16 [2048, 4096], P(('groups', 'seq'), 'chan'), parts along dimension 0, may hold values from -1.75 to 1.75
- filter_taps: bfloat16 [1024, 32], P('seq', 'chan'), may hold values from -6 to 6
- skip_gain: float32 [4096], P('chan'), may hold values from -1 to 1
Outputs:
- input_grad: bfloat16 [2048, 4096], P(('groups', 'seq'), 'chan'), parts along dimension 0
- filter_grad: float32 [2048, 32], P(('groups', 'seq'), 'chan'), parts along dimension 0
There are 2 independent parts, one for each index of `groups`. A program takes and returns all parts, laid end to end along the dimension named above; an argument that names none is the same for every part. Nothing has to cross between parts.
All inputs are finite; a program needn't handle non-finite values.
Results may differ from a plain program's by a relative error of at most 0.005.
Values may be sent and summed in bfloat16 or wider, within the bound.
No kernel may reach another device: no remote copies, remote signals or barrier semaphores. Data moves between devices by JAX's collectives and lax.ppermute only.
A program may use at most 64 MiB of HBM per device.

v0:
```python
import math
import jax
import jax.numpy as jnp
from jax import lax
from jax.sharding import PartitionSpec as P

lag_group = 4


def toeplitz_blocks(windows, block_rows):
    flipped = windows[..., ::-1]
    tiled = jnp.tile(flipped, (1, 1, block_rows))
    trimmed = tiled[..., : block_rows * (2 * block_rows - 1)]
    shaped = trimmed.reshape(windows.shape[0], windows.shape[1], block_rows, 2 * block_rows - 1)
    return shaped[..., block_rows - 1 : 2 * block_rows - 1]


def diagonal_sums(products, block_rows):
    flipped = products[..., ::-1]
    padded = jnp.pad(flipped, ((0, 0), (0, 0), (0, 0), (0, block_rows)))
    flattened = padded.reshape(products.shape[0], products.shape[1], 2 * block_rows * block_rows)
    trimmed = flattened[..., : block_rows * (2 * block_rows - 1)]
    shaped = trimmed.reshape(products.shape[0], products.shape[1], block_rows, 2 * block_rows - 1)
    diag_sums = jnp.sum(shaped, axis=2)
    return jnp.pad(diag_sums, ((0, 0), (0, 0), (1, 0)))


def fold_windows(window_grads, block_rows):
    front_half = jnp.pad(window_grads[..., :block_rows], ((0, 1), (0, 0), (0, 0)))
    back_half = jnp.pad(window_grads[..., block_rows:], ((1, 0), (0, 0), (0, 0)))
    joined = front_half + back_half
    return jnp.transpose(joined, (1, 0, 2)).reshape(window_grads.shape[1], -1)


def lag_table(taps_all, block_rows):
    return jnp.pad(jnp.transpose(taps_all), ((0, 0), (block_rows, lag_group * block_rows)))


def lag_sweep(
    blocks, base_block, block_count, sources, tap_table, block_rows, trip_count, seq_count
):
    filters = sources.shape[2]
    group_width = sources.shape[3]

    def advance(lag_step, state_pair):
        input_acc, lag_acc = state_pair
        lag_start = lag_step * lag_group
        stacked = jnp.stack(
            [
                lax.dynamic_slice_in_dim(blocks, base_block + lag_start + offset, block_count, 0)
                for offset in range(lag_group)
            ],
            axis=1,
        )
        lag_span = lax.dynamic_slice_in_dim(
            tap_table, lag_start * block_rows, (lag_group + 1) * block_rows, 1
        )
        windows = jnp.stack(
            [
                lag_span[:, offset * block_rows : (offset + 2) * block_rows]
                for offset in range(lag_group)
            ],
            axis=0,
        )
        toeplitz = toeplitz_blocks(windows, block_rows)
        input_acc = input_acc + jnp.einsum(
            "kfts,iktfg->isfg", toeplitz, stacked, preferred_element_type=jnp.float32
        )
        products = jnp.einsum(
            "iktfg,isfg->kfts", stacked, sources, preferred_element_type=jnp.float32
        )
        folded = fold_windows(diagonal_sums(products, block_rows), block_rows)
        previous = lax.dynamic_slice_in_dim(
            lag_acc, lag_start * block_rows, (lag_group + 1) * block_rows, 1
        )
        lag_acc = lax.dynamic_update_slice_in_dim(
            lag_acc, previous + folded, lag_start * block_rows, 1
        )
        return (input_acc, lag_acc)

    initial = (
        jnp.zeros((block_count, block_rows, filters, group_width), jnp.float32),
        jnp.zeros((filters, (seq_count + 1 + lag_group) * block_rows), jnp.float32),
    )
    return lax.fori_loop(0, trip_count, advance, initial)


def per_device(cached_input, cached_gate, out_grad, filter_taps, skip_gain):
    block_rows = cached_input.shape[0]
    chan_width = cached_input.shape[1]
    filters = filter_taps.shape[1]
    group_width = chan_width // filters
    seq_count = lax.axis_size("seq")
    seq_index = lax.axis_index("seq")
    length = block_rows * seq_count
    taps_scale = 1.0 / math.sqrt(length)
    gated_grad = (out_grad.astype(jnp.float32) * cached_gate.astype(jnp.float32)).astype(
        jnp.bfloat16
    )
    stretch_width = chan_width // seq_count
    moved_grad, moved_input = (
        lax.all_to_all(gated_grad, "seq", split_axis=1, concat_axis=0, tiled=True),
        lax.all_to_all(cached_input, "seq", split_axis=1, concat_axis=0, tiled=True),
    )
    taps_all = lax.all_gather(filter_taps, "seq", axis=0, tiled=True)
    stretch_filters = max(1, stretch_width // group_width)
    stretch_group = stretch_width // stretch_filters
    first_filter = seq_index * stretch_width // group_width
    stretch_taps = lax.dynamic_slice_in_dim(taps_all, first_filter, stretch_filters, 1)
    shaped_grad = moved_grad.reshape(seq_count, block_rows, stretch_filters, stretch_group)
    blocks = jnp.pad(shaped_grad, ((0, seq_count - 1 + lag_group), (0, 0), (0, 0), (0, 0)))
    sources = moved_input.reshape(seq_count, block_rows, stretch_filters, stretch_group)
    trip_count = (seq_count + lag_group - 1) // lag_group
    input_acc, lag_acc = lag_sweep(
        blocks,
        0,
        seq_count,
        sources,
        lag_table(stretch_taps, block_rows),
        block_rows,
        trip_count,
        seq_count,
    )
    stretch_gain = lax.dynamic_slice_in_dim(skip_gain, seq_index * stretch_width, stretch_width, 0)
    conv_grad = input_acc.reshape(length, stretch_width) * taps_scale
    local_grad = (conv_grad + stretch_gain[None, :] * moved_grad.astype(jnp.float32)).astype(
        jnp.bfloat16
    )
    input_grad = lax.all_to_all(local_grad, "seq", split_axis=0, concat_axis=1, tiled=True)
    stretch_term = jnp.transpose(lag_acc[:, block_rows : block_rows + length]) * taps_scale
    lag_term = lax.dynamic_update_slice_in_dim(
        jnp.zeros((length, filters), jnp.float32), stretch_term, first_filter, 1
    )
    filter_grad = lax.psum_scatter(lag_term, "seq", scatter_dimension=0, tiled=True)
    return (input_grad, filter_grad)


def solution(mesh):
    return jax.shard_map(
        per_device,
        mesh=mesh,
        in_specs=(
            P(("groups", "seq"), "chan"),
            P(("groups", "seq"), "chan"),
            P(("groups", "seq"), "chan"),
            P("seq", "chan"),
            P("chan"),
        ),
        out_specs=(P(("groups", "seq"), "chan"), P(("groups", "seq"), "chan")),
        check_vma=False,
    )
```

profile of v0, /device:TPU:0, one launch (start us, length us, event | category | flops | bytes accessed | tf_op | source)
XLA Modules:
  0.0 169.5 jit_solution(654285990207121783)
XLA Ops:
  7.2 1.3 multiply_convert_fusion
  8.5 1.0 copy.21
  9.5 7.3 %all-to-all-start = ((bf16[128,8,256]{0,2,1:T(8,128)(2,1)}), bf16[128,8,256]{0,2,1:T(8,128)(2,1)S(1)}, u32[]{:S(2)}, u32[]{:S(2)}) async-start(bf16[128,8,256]{0,2,1:T(8,128)(2,1)} %bitcast), calls=%async_computation | async-start | bytes 1048576 | tf_op jit(solution)/shard_map/all_to_all | solution.py:102
  16.8 1.0 copy.22
  17.8 13.4 %all-to-all-done = bf16[128,8,256]{0,2,1:T(8,128)(2,1)S(1)} async-done(((bf16[128,8,256]{0,2,1:T(8,128)(2,1)}), bf16[128,8,256]{0,2,1:T(8,128)(2,1)S(1)}, u32[]{:S(2)}, u32[]{:S(2)}) %all-to-all-start) | async-done | bytes 524320 | tf_op jit(solution)/shard_map/all_to_all | solution.py:102
  31.3 3.6 %all-to-all-start.1 = ((bf16[128,8,256]{0,2,1:T(8,128)(2,1)}), bf16[128,8,256]{0,2,1:T(8,128)(2,1)S(1)}, u32[]{:S(2)}, u32[]{:S(2)}) async-start(bf16[128,8,256]{0,2,1:T(8,128)(2,1)} %bitcast.4), calls=%async_computation.1 | async-start | bytes 1048576 | tf_op jit(solution)/shard_map/all_to_all | solution.py:103
  34.9 33.2 %all_gather.3 = bf16[1024,16]{0,1:T(8,128)(2,1)S(1)} all-gather(bf16[128,16]{0,1:T(8,128)(2,1)S(1)} %copy-done.7), channel_id=1, replica_groups=mesh['groups'=2,'seq'=8,'chan'=2] {'seq'}, dimensions={0}, use_global_device_ids=true | all-gather | bytes 36864 | tf_op jit(solution)/shard_map/all_gather | solution.py:105
  68.2 0.8 dynamic_slice.67
  69.0 0.2 pad.52.clone
  69.2 1.0 copy.24
  70.2 26.8 %while.18 = (s32[]{:T(128)}, f32[8,128,2,128]{1,3,0,2:T(8,128)}, f32[2,1664]{1,0:T(2,128)S(1)}, bf16[19,128,2,128]{1,3,0,2:T(8,128)(2,1)S(1)}, bf16[2,1664]{1,0:...) while((s32[]{:T(128)}, f32[8,128,2,128]{1,3,0,2:T(8,128)}, ...), condition=%wide.region_2.3_spmd.clone, body=%wide.region_0.2_spmd.clone.sunk | while | flops 543954432 | bytes 31783416 | solution.py:85
  70.2 1.2 dynamic-slice_bitcast_fusion.6
  71.4 0.2 rev.24
  71.7 0.1 tile.29
  71.8 0.4 slice.122
  72.2 1.6 reshape.89
  73.8 3.1 %fusion.19 = f32[8,128,2,128]{1,3,0,2:T(8,128)} fusion(f32[8,128,2,128]{1,3,0,2:T(8,128)} %get-tuple-element.301, pred[]{:T(512)S(6)} %compare.11, bf16[8,1,128,2,128]{2,4,1,0,3:T(8,128)(2,1)S(1)} %get-tuple-element.269, bf16[8,1,128,2,128]{2,4,1,0,3:T(8,128)(2,1)} %get-tuple-element.270, bf16[8,1,128,2,128]{2,4,1,0,3:T(8,128)(2,1)} %get-tuple-element.271, ...), kind=kOutput, calls=%fused_computation.2.clone.1 | convolution fusion | flops 272105472 | bytes 4456449 | tf_op jit(solution)/shard_map/while/body/eval_jaxpr/kfts,iktfg->isfg/dot_general | solution.py:66
  76.9 1.1 convolution_bitcast_fusion.3
  78.0 0.7 rev.25
  78.7 0.1 pad.116
  78.8 0.5 reshape.90
  79.4 1.1 slice.123
  80.4 2.8 %reshape.91 = f32[4,2,128,255]{3,2,0,1:T(8,128)S(1)} reshape(f32[4,2,32640]{2,0,1:T(4,128)} %slice.123) | data formatting | bytes 2088960 | tf_op jit(solution)/shard_map/while/body/eval_jaxpr/reshape | solution.py:23
  83.2 0.1 reduce_sum.18
  83.4 0.1 pad_slice_fusion.2
  83.5 1.2 dynamic-slice_bitcast_fusion.6
  84.7 0.2 rev.24
  85.0 0.1 tile.29
  85.1 0.4 slice.122
  85.5 1.6 reshape.89
  87.1 3.4 %fusion.19 = f32[8,128,2,128]{1,3,0,2:T(8,128)} fusion(f32[8,128,2,128]{1,3,0,2:T(8,128)} %get-tuple-element.301, pred[]{:T(512)S(6)} %compare.11, bf16[8,1,128,2,128]{2,4,1,0,3:T(8,128)(2,1)S(1)} %get-tuple-element.269, bf16[8,1,128,2,128]{2,4,1,0,3:T(8,128)(2,1)} %get-tuple-element.270, bf16[8,1,128,2,128]{2,4,1,0,3:T(8,128)(2,1)} %get-tuple-element.271, ...), kind=kOutput, calls=%fused_computation.2.clone.1 | convolution fusion | flops 272105472 | bytes 4456449 | tf_op jit(solution)/shard_map/while/body/eval_jaxpr/kfts,iktfg->isfg/dot_general | solution.py:66
  90.5 1.1 convolution_bitcast_fusion.3
  91.6 0.7 rev.25
  92.3 0.1 pad.116
  92.5 0.5 reshape.90
  93.0 1.1 slice.123
  94.0 2.8 %reshape.91 = f32[4,2,128,255]{3,2,0,1:T(8,128)S(1)} reshape(f32[4,2,32640]{2,0,1:T(4,128)} %slice.123) | data formatting | bytes 2088960 | tf_op jit(solution)/shard_map/while/body/eval_jaxpr/reshape | solution.py:23
  96.9 0.1 reduce_sum.18
  97.0 0.1 pad_slice_fusion.2
  97.1 1.4 copy_multiply_fusion
  98.5 1.0 fusion.9
  99.5 3.5 %all-to-all-start.2 = ((bf16[8,128,256]{1,2,0:T(8,128)(2,1)}), bf16[8,128,256]{1,2,0:T(8,128)(2,1)S(1)}, u32[]{:S(2)}, u32[]{:S(2)}) async-start(bf16[8,128,256]{1,2,0:T(8,128)(2,1)} %fusion.9), calls=%async_computation.2 | async-start | bytes 1048576 | tf_op jit(solution)/shard_map/all_to_all | solution.py:129
  103.0 0.0 reduce-scatter.2.cloned.1.call-start
  103.0 0.3 dynamic_update_slice.13
  103.4 0.6 copy-done.6
  104.0 9.2 %all-to-all-done.2 = bf16[8,128,256]{1,2,0:T(8,128)(2,1)S(1)} async-done(((bf16[8,128,256]{1,2,0:T(8,128)(2,1)}), bf16[8,128,256]{1,2,0:T(8,128)(2,1)S(1)}, u32[]{:S(2)}, u32[]{:S(2)}) %all-to-all-start.2) | async-done | bytes 524320 | tf_op jit(solution)/shard_map/all_to_all | solution.py:129
  113.2 1.0 copy.26
  114.2 48.4 %reduce-scatter.2.cloned.1.call-done = f32[128,16]{0,1:T(8,128)} async-done(((f32[1024,16]{0,1:T(8,128)}), f32[128,16]{0,1:T(8,128)}) %reduce-scatter.2.cloned.1.call-update) | async-done | bytes 8208 | tf_op jit(solution)/shard_map/reduce_scatter | solution.py:134
  (40 shorter events, 0.3 us)
Async XLA Ops:
  8.5 8.3 %copy-start.4 = (bf16[128,2048]{1,0:T(8,128)(2,1)S(1)}, bf16[128,2048]{1,0:T(8,128)(2,1)}, u32[]{:S(2)}) copy-start(bf16[128,2048]{1,0:T(8,128)(2,1)} %param.7) | copy-start | bytes 1572868
  9.5 21.8 %all-to-all-start = ((bf16[128,8,256]{0,2,1:T(8,128)(2,1)}), bf16[128,8,256]{0,2,1:T(8,128)(2,1)S(1)}, u32[]{:S(2)}, u32[]{:S(2)}) async-start(bf16[128,8,256]{0,2,1:T(8,128)(2,1)} %bitcast), calls=%async_computation | async-start | bytes 1048576 | tf_op jit(solution)/shard_map/all_to_all | solution.py:102
  16.8 18.1 %copy-start.7 = (bf16[128,16]{0,1:T(8,128)(2,1)S(1)}, bf16[128,16]{0,1:T(8,128)(2,1)}, u32[]{:S(2)}) copy-start(bf16[128,16]{0,1:T(8,128)(2,1)} %param.10) | copy-start | bytes 12292
  31.3 37.6 %copy-start.2 = (bf16[128,8,256]{0,2,1:T(8,128)(2,1)}, bf16[128,8,256]{0,2,1:T(8,128)(2,1)S(1)}, u32[]{:S(2)}) copy-start(bf16[128,8,256]{0,2,1:T(8,128)(2,1)S(1)} %all-to-all-done) | copy-start | bytes 1572868
  31.3 37.9 %all-to-all-start.1 = ((bf16[128,8,256]{0,2,1:T(8,128)(2,1)}), bf16[128,8,256]{0,2,1:T(8,128)(2,1)S(1)}, u32[]{:S(2)}, u32[]{:S(2)}) async-start(bf16[128,8,256]{0,2,1:T(8,128)(2,1)} %bitcast.4), calls=%async_computation.1 | async-start | bytes 1048576 | tf_op jit(solution)/shard_map/all_to_all | solution.py:103
  73.7 3.1 %copy-start = (bf16[8,1,128,2,128]{2,4,1,0,3:T(8,128)(2,1)S(1)}, bf16[8,1,128,2,128]{2,4,1,0,3:T(8,128)(2,1)}, u32[]{:S(2)}) copy-start(bf16[8,1,128,2,128]{2,4,1,0,3:T(8,128)(2,1)} %get-tuple-element.270) | copy-start | bytes 1572868 | tf_op jit(solution)/shard_map/while
  73.8 3.1 %copy-start.1 = (bf16[8,1,128,2,128]{2,4,1,0,3:T(8,128)(2,1)S(1)}, bf16[8,1,128,2,128]{2,4,1,0,3:T(8,128)(2,1)}, u32[]{:S(2)}) copy-start(bf16[8,1,128,2,128]{2,4,1,0,3:T(8,128)(2,1)} %get-tuple-element.271) | copy-start | bytes 1572868 | tf_op jit(solution)/shard_map/while
  73.8 3.1 %copy-start.5 = (bf16[8,128,2,128]{3,1,0,2:T(8,128)(2,1)S(1)}, bf16[8,128,2,128]{3,1,0,2:T(8,128)(2,1)}, u32[]{:S(2)}) copy-start(bf16[8,128,2,128]{3,1,0,2:T(8,128)(2,1)} %get-tuple-element.326) | copy-start | bytes 1572868 | tf_op jit(solution)/shard_map/while
  87.0 3.5 %copy-start = (bf16[8,1,128,2,128]{2,4,1,0,3:T(8,128)(2,1)S(1)}, bf16[8,1,128,2,128]{2,4,1,0,3:T(8,128)(2,1)}, u32[]{:S(2)}) copy-start(bf16[8,1,128,2,128]{2,4,1,0,3:T(8,128)(2,1)} %get-tuple-element.270) | copy-start | bytes 1572868 | tf_op jit(solution)/shard_map/while
  87.0 3.5 %copy-start.1 = (bf16[8,1,128,2,128]{2,4,1,0,3:T(8,128)(2,1)S(1)}, bf16[8,1,128,2,128]{2,4,1,0,3:T(8,128)(2,1)}, u32[]{:S(2)}) copy-start(bf16[8,1,128,2,128]{2,4,1,0,3:T(8,128)(2,1)} %get-tuple-element.271) | copy-start | bytes 1572868 | tf_op jit(solution)/shard_map/while
  87.0 3.5 %copy-start.5 = (bf16[8,128,2,128]{3,1,0,2:T(8,128)(2,1)S(1)}, bf16[8,128,2,128]{3,1,0,2:T(8,128)(2,1)}, u32[]{:S(2)}) copy-start(bf16[8,128,2,128]{3,1,0,2:T(8,128)(2,1)} %get-tuple-element.326) | copy-start | bytes 1572868 | tf_op jit(solution)/shard_map/while
  97.1 1.4 copy-start.3
  99.5 13.8 %all-to-all-start.2 = ((bf16[8,128,256]{1,2,0:T(8,128)(2,1)}), bf16[8,128,256]{1,2,0:T(8,128)(2,1)S(1)}, u32[]{:S(2)}, u32[]{:S(2)}) async-start(bf16[8,128,256]{1,2,0:T(8,128)(2,1)} %fusion.9), calls=%async_computation.2 | async-start | bytes 1048576 | tf_op jit(solution)/shard_map/all_to_all | solution.py:129
  103.0 59.7 %reduce-scatter.2.cloned.1.call-start = ((), (), s32[]{:S(2)}) async-start(), calls=%async_computation.4 | async-start | bytes 73728 | tf_op jit(solution)/shard_map/reduce_scatter | solution.py:134
  103.3 0.6 copy-start.6
Sparse Core Ops, SparseCore 0:
  107.5 55.0 reduce-scatter.1
where the time goes:
time: 170 us; the launch traced here: 169 us
  waiting for transfers between devices  71.1 us (42%)
  blocking collectives  33.2 us (20%)
  local copies, waits for them, and re-layouts  23.6 us (14%)
  starting transfers between devices  14.5 us (9%)
  between operations  14.2 us (8%)
  matrix products  8.75 us (5%)
  other arithmetic  3.94 us (2%)
    reduce_scatter x1, waiting for transfers between devices, per_device(): lax.psum_scatter(lag_term, 'seq', scatter_dimension=0, tiled=True)  48.4 us
    all_gather x1, blocking collectives, per_device(): taps_all = lax.all_gather(filter_taps, 'seq', axis=0, tiled=True)  33.2 us
    all_to_all x1, waiting for transfers between devices, per_device(): lax.all_to_all(gated_grad, 'seq', split_axis=1, concat_axis=0, tiled=True)  13.4 us
    all_to_all x1, waiting for transfers between devices, per_device(): lax.all_to_all(local_grad, 'seq', split_axis=0, concat_axis=1, tiled=True)  9.23 us
    all_to_all x1, starting transfers between devices, per_device(): lax.all_to_all(gated_grad, 'seq', split_axis=1, concat_axis=0, tiled=True)  7.28 us
    dot_general x2, matrix products, advance(): jnp.einsum('kfts,iktfg->isfg', toeplitz, stacked, preferred_element_type=...  6.53 us
    reshape x2, local copies, waits for them, and re-layouts, diagonal_sums(): trimmed.reshape(products.shape[0], products.shape[1], block_rows, 2 * blo...  5.62 us
    unnamed x14, local copies, waits for them, and re-layouts  3.72 us
  transfers between devices with their start and end apart: 4, of which 3 were waited for; matrix products, arithmetic and copies ran while one was open for 2% of the time, Pallas kernels for 0%

commit v1 on v0

--- a/solution.py
+++ b/solution.py
@@ -5,6 +5,22 @@
 from jax.sharding import PartitionSpec as P
 
 lag_group = 4
+
+
+def run_inputs(state):
+    chip_axis = "seq"
+    piece_now, finding = (lax.psum(1, chip_axis), lax.axis_index(chip_axis))
+    part_next, p_next = (state, 1)
+    while p_next < piece_now:
+        fields = []
+        for u in range(piece_now):
+            fields.append((u, u ^ p_next))
+        even = lax.ppermute(part_next, chip_axis, fields)
+        step_out = jnp.concatenate([part_next, even], 0)
+        arr_out = jnp.concatenate([even, part_next], 0)
+        part_next = jnp.where(finding & p_next == 0, step_out, arr_out)
+        p_next = 2 * p_next
+    return part_next
 
 
 def toeplitz_blocks(windows, block_rows):
@@ -102,7 +118,7 @@
         lax.all_to_all(gated_grad, "seq", split_axis=1, concat_axis=0, tiled=True),
         lax.all_to_all(cached_input, "seq", split_axis=1, concat_axis=0, tiled=True),
     )
-    taps_all = lax.all_gather(filter_taps, "seq", axis=0, tiled=True)
+    taps_all = run_inputs(filter_taps)
     stretch_filters = max(1, stretch_width // group_width)
     stretch_group = stretch_width // stretch_filters
     first_filter = seq_index * stretch_width // group_width

time: 170 us -> 153 us (0.900)
  blocking collectives: 33.2 us -> 0 us
  starting transfers between devices: 14.5 us -> 22.9 us
  waiting for transfers between devices: 71.1 us -> 78.8 us
    all_gather x1 -> x0, blocking collectives: 33.2 us -> none  [per_device(): taps_all = lax.all_gather(filter_taps, 'seq', axis=0, tiled=True)]
    ppermute x0 -> x3, waiting for transfers between devices: none -> 7.67 us  [run_inputs(): even = lax.ppermute(part_next, chip_axis, fields)]
    ppermute x0 -> x3, starting transfers between devices: none -> 6.82 us  [run_inputs(): even = lax.ppermute(part_next, chip_axis, fields)]
    all_to_all x1, waiting for transfers between devices: 9.23 us -> 11.8 us  [per_device(): lax.all_to_all(local_grad, 'seq', split_axis=0, concat_axis=1, tiled=True)]
    reduce_scatter x1, waiting for transfers between devices: 48.4 us -> 45.9 us  [per_device(): lax.psum_scatter(lag_term, 'seq', scatter_dimension=0, tiled=True)]
  transfers between devices with their start and end apart: 4 -> 7, of which waited for: 3 -> 6; matrix products, arithmetic and copies ran while one was open for 2% -> 2% of each run, Pallas kernels for 0% -> 0%
where the time goes in v1:
time: 153 us; the launch traced here: 152 us
  waiting for transfers between devices  78.8 us (52%)
  local copies, waits for them, and re-layouts  23.6 us (15%)
  starting transfers between devices  22.9 us (15%)
  between operations  14.2 us (9%)
  matrix products  8.76 us (6%)
  other arithmetic  3.99 us (3%)
    reduce_scatter x1, waiting for transfers between devices, per_device(): lax.psum_scatter(lag_term, 'seq', scatter_dimension=0, tiled=True)  45.9 us
    all_to_all x1, waiting for transfers between devices, per_device(): lax.all_to_all(gated_grad, 'seq', split_axis=1, concat_axis=0, tiled=True)  13.4 us
    all_to_all x1, waiting for transfers between devices, per_device(): lax.all_to_all(local_grad, 'seq', split_axis=0, concat_axis=1, tiled=True)  11.8 us
    ppermute x3, waiting for transfers between devices, run_inputs(): even = lax.ppermute(part_next, chip_axis, fields)  7.67 us
    all_to_all x1, starting transfers between devices, per_device(): lax.all_to_all(gated_grad, 'seq', split_axis=1, concat_axis=0, tiled=True)  7.28 us
    ppermute x3, starting transfers between devices, run_inputs(): even = lax.ppermute(part_next, chip_axis, fields)  6.82 us
    dot_general x2, matrix products, advance(): jnp.einsum('kfts,iktfg->isfg', toeplitz, stacked, preferred_element_type=...  6.54 us
    reshape x2, local copies, waits for them, and re-layouts, diagonal_sums(): trimmed.reshape(products.shape[0], products.shape[1], block_rows, 2 * blo...  5.62 us
  transfers between devices with their start and end apart: 7, of which 6 were waited for; matrix products, arithmetic and copies ran while one was open for 2% of the time, Pallas kernels for 0%

profile of v1, /device:TPU:0, one launch (start us, length us, event | category | flops | bytes accessed | tf_op | source)
XLA Modules:
  0.0 152.5 jit_solution(509034260542738656)
XLA Ops:
  7.2 1.3 multiply_convert_fusion
  8.5 1.0 copy.21
  9.5 7.3 %all-to-all-start = ((bf16[128,8,256]{0,2,1:T(8,128)(2,1)}), bf16[128,8,256]{0,2,1:T(8,128)(2,1)S(1)}, u32[]{:S(2)}, u32[]{:S(2)}) async-start(bf16[128,8,256]{0,2,1:T(8,128)(2,1)} %bitcast), calls=%async_computation | async-start | bytes 1048576 | tf_op jit(solution)/shard_map/all_to_all | solution.py:118
  16.8 1.0 copy.22
  17.8 13.4 %all-to-all-done = bf16[128,8,256]{0,2,1:T(8,128)(2,1)S(1)} async-done(((bf16[128,8,256]{0,2,1:T(8,128)(2,1)}), bf16[128,8,256]{0,2,1:T(8,128)(2,1)S(1)}, u32[]{:S(2)}, u32[]{:S(2)}) %all-to-all-start) | async-done | bytes 524320 | tf_op jit(solution)/shard_map/all_to_all | solution.py:118
  31.3 3.6 %all-to-all-start.1 = ((bf16[128,8,256]{0,2,1:T(8,128)(2,1)}), bf16[128,8,256]{0,2,1:T(8,128)(2,1)S(1)}, u32[]{:S(2)}, u32[]{:S(2)}) async-start(bf16[128,8,256]{0,2,1:T(8,128)(2,1)} %bitcast.4), calls=%async_computation.1 | async-start | bytes 1048576 | tf_op jit(solution)/shard_map/all_to_all | solution.py:119
  34.9 2.0 %collective-permute-start = (bf16[128,16]{0,1:T(8,128)(2,1)S(1)}, bf16[128,16]{0,1:T(8,128)(2,1)S(1)}, u32[]{:S(2)}, u32[]{:S(2)}) collective-permute-start(bf16[128,16]{0,1:T(8,128)(2,1)S(1)} %copy-done.7), channel_id=1, source_target_pairs={{0,2},{2,0},{4,6},{6,4},{8,10},{10,8},{12,14},{14,12},{1,3},{3,1},... | collective-permute-start | bytes 12296 | tf_op jit(solution)/shard_map/ppermute | solution.py:18
  36.9 3.8 %collective-permute-done = bf16[128,16]{0,1:T(8,128)(2,1)S(1)} collective-permute-done((bf16[128,16]{0,1:T(8,128)(2,1)S(1)}, bf16[128,16]{0,1:T(8,128)(2,1)S(1)}, u32[]{:S(2)}, u32[]{:S(2)}) %collective-permute-start) | collective-permute-done | bytes 4128 | tf_op jit(solution)/shard_map/ppermute | solution.py:18
  40.8 0.8 collective-permute-start.1
  41.6 2.9 %collective-permute-done.1 = bf16[256,16]{0,1:T(8,128)(2,1)S(1)} collective-permute-done((bf16[256,16]{0,1:T(8,128)(2,1)S(1)}, bf16[256,16]{0,1:T(8,128)(2,1)S(1)}, u32[]{:S(2)}, u32[]{:S(2)}) %collective-permute-start.1) | collective-permute-done | bytes 8224 | tf_op jit(solution)/shard_map/ppermute | solution.py:18
  44.5 4.0 %collective-permute-start.2 = (bf16[512,16]{0,1:T(8,128)(2,1)S(1)}, bf16[512,16]{0,1:T(8,128)(2,1)S(1)}, u32[]{:S(2)}, u32[]{:S(2)}) collective-permute-start(bf16[512,16]{0,1:T(8,128)(2,1)S(1)} %maximum_select_fusion), channel_id=1, source_target_pairs={{0,8},{2,10},{4,12},{6,14},{8,0},{10,2},{12,4},{14,6},{1,9},{3,11}... | collective-permute-start | bytes 49160 | tf_op jit(solution)/shard_map/ppermute | solution.py:18
  48.5 0.8 dynamic_slice.67
  49.2 1.0 collective-permute-done.2
  50.3 0.2 pad.52.clone
  50.5 1.0 copy.24
  51.5 26.9 %while.18 = (s32[]{:T(128)}, f32[8,128,2,128]{1,3,0,2:T(8,128)}, f32[2,1664]{1,0:T(2,128)S(1)}, bf16[19,128,2,128]{1,3,0,2:T(8,128)(2,1)S(1)}, bf16[2,1664]{1,0:...) while((s32[]{:T(128)}, f32[8,128,2,128]{1,3,0,2:T(8,128)}, ...), condition=%wide.region_2.3_spmd.clone, body=%wide.region_0.2_spmd.clone.sunk | while | flops 543954432 | bytes 31783416 | solution.py:101
  51.5 1.2 dynamic-slice_bitcast_fusion.5
  52.8 0.2 rev.24
  53.0 0.1 tile.29
  53.1 0.4 slice.122
  53.5 1.6 %reshape.89 = bf16[4,2,128,255]{3,2,1,0:T(8,128)(2,1)S(1)} reshape(bf16[4,2,32640]{2,1,0:T(2,128)(2,1)S(1)} %slice.122) | data formatting | bytes 1044480 | tf_op jit(solution)/shard_map/while/body/eval_jaxpr/reshape | solution.py:30
  55.1 3.1 %fusion.22 = f32[8,128,2,128]{1,3,0,2:T(8,128)} fusion(f32[8,128,2,128]{1,3,0,2:T(8,128)} %get-tuple-element.301, pred[]{:T(512)S(6)} %compare.11, bf16[8,1,128,2,128]{2,4,1,0,3:T(8,128)(2,1)S(1)} %get-tuple-element.269, bf16[8,1,128,2,128]{2,4,1,0,3:T(8,128)(2,1)} %get-tuple-element.270, bf16[8,1,128,2,128]{2,4,1,0,3:T(8,128)(2,1)} %get-tuple-element.271, ...), kind=kOutput, calls=%fused_computation.2.clone.1 | convolution fusion | flops 272105472 | bytes 4456449 | tf_op jit(solution)/shard_map/while/body/eval_jaxpr/kfts,iktfg->isfg/dot_general | solution.py:82
  58.2 1.1 convolution_bitcast_fusion.3
  59.3 0.7 rev.25
  60.1 0.1 pad.164
  60.2 0.5 reshape.90
  60.7 1.1 slice.123
  61.8 2.8 %reshape.91 = f32[4,2,128,255]{3,2,0,1:T(8,128)S(1)} reshape(f32[4,2,32640]{2,0,1:T(4,128)} %slice.123) | data formatting | bytes 2088960 | tf_op jit(solution)/shard_map/while/body/eval_jaxpr/reshape | solution.py:39
  64.8 1.2 dynamic-slice_bitcast_fusion.5
  66.1 0.2 rev.24
  66.3 0.1 tile.29
  66.4 0.4 slice.122
  66.8 1.6 %reshape.89 = bf16[4,2,128,255]{3,2,1,0:T(8,128)(2,1)S(1)} reshape(bf16[4,2,32640]{2,1,0:T(2,128)(2,1)S(1)} %slice.122) | data formatting | bytes 1044480 | tf_op jit(solution)/shard_map/while/body/eval_jaxpr/reshape | solution.py:30
  68.4 3.4 %fusion.22 = f32[8,128,2,128]{1,3,0,2:T(8,128)} fusion(f32[8,128,2,128]{1,3,0,2:T(8,128)} %get-tuple-element.301, pred[]{:T(512)S(6)} %compare.11, bf16[8,1,128,2,128]{2,4,1,0,3:T(8,128)(2,1)S(1)} %get-tuple-element.269, bf16[8,1,128,2,128]{2,4,1,0,3:T(8,128)(2,1)} %get-tuple-element.270, bf16[8,1,128,2,128]{2,4,1,0,3:T(8,128)(2,1)} %get-tuple-element.271, ...), kind=kOutput, calls=%fused_computation.2.clone.1 | convolution fusion | flops 272105472 | bytes 4456449 | tf_op jit(solution)/shard_map/while/body/eval_jaxpr/kfts,iktfg->isfg/dot_general | solution.py:82
  71.9 1.1 convolution_bitcast_fusion.3
  73.0 0.7 rev.25
  73.7 0.1 pad.164
  73.8 0.5 reshape.90
  74.3 1.1 slice.123
  75.4 2.8 %reshape.91 = f32[4,2,128,255]{3,2,0,1:T(8,128)S(1)} reshape(f32[4,2,32640]{2,0,1:T(4,128)} %slice.123) | data formatting | bytes 2088960 | tf_op jit(solution)/shard_map/while/body/eval_jaxpr/reshape | solution.py:39
  78.4 1.4 copy_multiply_fusion
  79.8 1.0 fusion.9
  80.8 5.1 %all-to-all-start.2 = ((bf16[8,128,256]{1,2,0:T(8,128)(2,1)}), bf16[8,128,256]{1,2,0:T(8,128)(2,1)S(1)}, u32[]{:S(2)}, u32[]{:S(2)}) async-start(bf16[8,128,256]{1,2,0:T(8,128)(2,1)} %fusion.9), calls=%async_computation.2 | async-start | bytes 1048576 | tf_op jit(solution)/shard_map/all_to_all | solution.py:145
  86.0 0.3 dynamic_update_slice.13
  86.4 0.6 copy-done.6
  87.0 11.8 %all-to-all-done.2 = bf16[8,128,256]{1,2,0:T(8,128)(2,1)S(1)} async-done(((bf16[8,128,256]{1,2,0:T(8,128)(2,1)}), bf16[8,128,256]{1,2,0:T(8,128)(2,1)S(1)}, u32[]{:S(2)}, u32[]{:S(2)}) %all-to-all-start.2) | async-done | bytes 524320 | tf_op jit(solution)/shard_map/all_to_all | solution.py:145
  98.8 1.0 copy.26
  99.8 45.9 %reduce-scatter.2.cloned.1.call-done = f32[128,16]{0,1:T(8,128)} async-done(((f32[1024,16]{0,1:T(8,128)}), f32[128,16]{0,1:T(8,128)}) %reduce-scatter.2.cloned.1.call-update) | async-done | bytes 8208 | tf_op jit(solution)/shard_map/reduce_scatter | solution.py:150
  (47 shorter events, 0.7 us)
Async XLA Ops:
  8.5 8.3 %copy-start.4 = (bf16[128,2048]{1,0:T(8,128)(2,1)S(1)}, bf16[128,2048]{1,0:T(8,128)(2,1)}, u32[]{:S(2)}) copy-start(bf16[128,2048]{1,0:T(8,128)(2,1)} %param.7) | copy-start | bytes 1572868
  9.5 21.8 %all-to-all-start = ((bf16[128,8,256]{0,2,1:T(8,128)(2,1)}), bf16[128,8,256]{0,2,1:T(8,128)(2,1)S(1)}, u32[]{:S(2)}, u32[]{:S(2)}) async-start(bf16[128,8,256]{0,2,1:T(8,128)(2,1)} %bitcast), calls=%async_computation | async-start | bytes 1048576 | tf_op jit(solution)/shard_map/all_to_all | solution.py:118
  16.8 18.1 %copy-start.7 = (bf16[128,16]{0,1:T(8,128)(2,1)S(1)}, bf16[128,16]{0,1:T(8,128)(2,1)}, u32[]{:S(2)}) copy-start(bf16[128,16]{0,1:T(8,128)(2,1)} %param.10) | copy-start | bytes 12292
  31.3 19.0 %copy-start.2 = (bf16[128,8,256]{0,2,1:T(8,128)(2,1)}, bf16[128,8,256]{0,2,1:T(8,128)(2,1)S(1)}, u32[]{:S(2)}) copy-start(bf16[128,8,256]{0,2,1:T(8,128)(2,1)S(1)} %all-to-all-done) | copy-start | bytes 1572868
  31.3 19.2 %all-to-all-start.1 = ((bf16[128,8,256]{0,2,1:T(8,128)(2,1)}), bf16[128,8,256]{0,2,1:T(8,128)(2,1)S(1)}, u32[]{:S(2)}, u32[]{:S(2)}) async-start(bf16[128,8,256]{0,2,1:T(8,128)(2,1)} %bitcast.4), calls=%async_computation.1 | async-start | bytes 1048576 | tf_op jit(solution)/shard_map/all_to_all | solution.py:119
  34.9 5.9 %collective-permute-start = (bf16[128,16]{0,1:T(8,128)(2,1)S(1)}, bf16[128,16]{0,1:T(8,128)(2,1)S(1)}, u32[]{:S(2)}, u32[]{:S(2)}) collective-permute-start(bf16[128,16]{0,1:T(8,128)(2,1)S(1)} %copy-done.7), channel_id=1, source_target_pairs={{0,2},{2,0},{4,6},{6,4},{8,10},{10,8},{12,14},{14,12},{1,3},{3,1},... | collective-permute-start | bytes 12296 | tf_op jit(solution)/shard_map/ppermute | solution.py:18
  40.8 3.7 %collective-permute-start.1 = (bf16[256,16]{0,1:T(8,128)(2,1)S(1)}, bf16[256,16]{0,1:T(8,128)(2,1)S(1)}, u32[]{:S(2)}, u32[]{:S(2)}) collective-permute-start(bf16[256,16]{0,1:T(8,128)(2,1)S(1)} %maximum_select_fusion.1), channel_id=1, source_target_pairs={{0,4},{2,6},{4,0},{6,2},{8,12},{10,14},{12,8},{14,10},{1,5},{3,7},... | collective-permute-start | bytes 24584 | tf_op jit(solution)/shard_map/ppermute | solution.py:18
  44.5 5.7 %collective-permute-start.2 = (bf16[512,16]{0,1:T(8,128)(2,1)S(1)}, bf16[512,16]{0,1:T(8,128)(2,1)S(1)}, u32[]{:S(2)}, u32[]{:S(2)}) collective-permute-start(bf16[512,16]{0,1:T(8,128)(2,1)S(1)} %maximum_select_fusion), channel_id=1, source_target_pairs={{0,8},{2,10},{4,12},{6,14},{8,0},{10,2},{12,4},{14,6},{1,9},{3,11}... | collective-permute-start | bytes 49160 | tf_op jit(solution)/shard_map/ppermute | solution.py:18
  55.1 3.1 %copy-start = (bf16[8,1,128,2,128]{2,4,1,0,3:T(8,128)(2,1)S(1)}, bf16[8,1,128,2,128]{2,4,1,0,3:T(8,128)(2,1)}, u32[]{:S(2)}) copy-start(bf16[8,1,128,2,128]{2,4,1,0,3:T(8,128)(2,1)} %get-tuple-element.270) | copy-start | bytes 1572868 | tf_op jit(solution)/shard_map/while
  55.1 3.1 %copy-start.1 = (bf16[8,1,128,2,128]{2,4,1,0,3:T(8,128)(2,1)S(1)}, bf16[8,1,128,2,128]{2,4,1,0,3:T(8,128)(2,1)}, u32[]{:S(2)}) copy-start(bf16[8,1,128,2,128]{2,4,1,0,3:T(8,128)(2,1)} %get-tuple-element.271) | copy-start | bytes 1572868 | tf_op jit(solution)/shard_map/while
  55.1 3.1 %copy-start.5 = (bf16[8,128,2,128]{3,1,0,2:T(8,128)(2,1)S(1)}, bf16[8,128,2,128]{3,1,0,2:T(8,128)(2,1)}, u32[]{:S(2)}) copy-start(bf16[8,128,2,128]{3,1,0,2:T(8,128)(2,1)} %get-tuple-element.326) | copy-start | bytes 1572868 | tf_op jit(solution)/shard_map/while
  68.4 3.5 %copy-start = (bf16[8,1,128,2,128]{2,4,1,0,3:T(8,128)(2,1)S(1)}, bf16[8,1,128,2,128]{2,4,1,0,3:T(8,128)(2,1)}, u32[]{:S(2)}) copy-start(bf16[8,1,128,2,128]{2,4,1,0,3:T(8,128)(2,1)} %get-tuple-element.270) | copy-start | bytes 1572868 | tf_op jit(solution)/shard_map/while
  68.4 3.5 %copy-start.1 = (bf16[8,1,128,2,128]{2,4,1,0,3:T(8,128)(2,1)S(1)}, bf16[8,1,128,2,128]{2,4,1,0,3:T(8,128)(2,1)}, u32[]{:S(2)}) copy-start(bf16[8,1,128,2,128]{2,4,1,0,3:T(8,128)(2,1)} %get-tuple-element.271) | copy-start | bytes 1572868 | tf_op jit(solution)/shard_map/while
  68.4 3.5 %copy-start.5 = (bf16[8,128,2,128]{3,1,0,2:T(8,128)(2,1)S(1)}, bf16[8,128,2,128]{3,1,0,2:T(8,128)(2,1)}, u32[]{:S(2)}) copy-start(bf16[8,128,2,128]{3,1,0,2:T(8,128)(2,1)} %get-tuple-element.326) | copy-start | bytes 1572868 | tf_op jit(solution)/shard_map/while
  78.4 1.4 copy-start.3
  80.8 17.9 %all-to-all-start.2 = ((bf16[8,128,256]{1,2,0:T(8,128)(2,1)}), bf16[8,128,256]{1,2,0:T(8,128)(2,1)S(1)}, u32[]{:S(2)}, u32[]{:S(2)}) async-start(bf16[8,128,256]{1,2,0:T(8,128)(2,1)} %fusion.9), calls=%async_computation.2 | async-start | bytes 1048576 | tf_op jit(solution)/shard_map/all_to_all | solution.py:145
  86.0 59.7 %reduce-scatter.2.cloned.1.call-start = ((), (), s32[]{:S(2)}) async-start(), calls=%async_computation.4 | async-start | bytes 73728 | tf_op jit(solution)/shard_map/reduce_scatter | solution.py:150
  86.4 0.6 copy-start.6
Sparse Core Ops, SparseCore 0:
  90.5 55.1 reduce-scatter.1
